TPU v7x, 32 devices: a whole 2x2x4 slice. The times are simulated.
32 devices in a mesh: dp: 2 (over x), mp: 16 (over z, y, core).
Axes of the slice: x: 2, y: 2, z: 4, core: 2. Of those that a mesh axis runs over, the one named last changes fastest.
Arguments:
- node_features: bfloat16 [512, 6144], P('mp', 'dp'), may hold values from -6 to 6
- weights_one: bfloat16 [1024, 512], replicated, may hold values from -0.25 to 0.25
- weights_two: bfloat16 [1024, 512], replicated, may hold values from -0.25 to 0.25
- neighbor_owner: int32 [6144, 8], P('dp'), may hold values from 0 to 15, all different within a row; in each aligned block of 192 rows (0 to 191, 192 to 383, ...) at most 144 rows name the same one
- neighbor_row: int32 [6144, 8], P('dp'), may hold values from 0 to 191
- neighbor_count: int32 [6144], P('dp'), may hold values from 4 to 8
- cotangent: bfloat16 [6144, 512], P(('dp', 'mp')), may hold values from -0.076171875 to 0.076171875
Outputs:
- node_output: bfloat16 [6144, 512], P(('dp', 'mp'))
- weight_grads: float32 [2048, 512], P(('dp', 'mp'))
Inputs may be any that keep to these rules, and one draw needn't show every extreme that they name: `neighbor_owner`: each row names 8 different owners; among the rows of one device (aligned blocks of 192 rows) no owner is named more than 144 times, and in some block one owner exactly 144 times. Slots k >= neighbor_count[r] are padding and carry no edge.
All inputs are finite; a program needn't handle non-finite values.
Results may differ from a plain program's by a relative error of at most 0.0052.
Values may be sent and summed in bfloat16 or wider, within the bound.
No kernel may reach another device: no remote copies, remote signals or barrier semaphores. Data moves between devices by JAX's collectives and lax.ppermute only.
A program may use at most 64 MiB of HBM per device.

v0:
```python
import jax
import jax.numpy as jnp
from jax import lax
from jax.sharding import PartitionSpec as P


def column_mean(table, indices, live, inverse):
    total = jnp.zeros((table.shape[0], indices.shape[1]), jnp.float32)
    for slot_index in range(indices.shape[0]):
        picked = jnp.take(table, indices[slot_index], axis=1)
        kept = jnp.where(live[slot_index][None, :], picked, jnp.zeros_like(picked))
        total = total + kept.astype(jnp.float32)
    return (total * inverse[None, :]).astype(jnp.bfloat16)


def silu_slope(values):
    sigmoid = jax.nn.sigmoid(values)
    return sigmoid * (1.0 + values * (1.0 - sigmoid))


def contract(left, right, left_dim, right_dim):
    return lax.dot_general(
        left, right, (((left_dim,), (right_dim,)), ((), ())), preferred_element_type=jnp.float32
    )


def swap(values, axis, mask):
    size = lax.axis_size(axis)
    return lax.ppermute(values, axis, [(j, j ^ mask) for j in range(size)])


def halving_scatter(terms, order):
    n_mp = lax.axis_size("mp")
    top = n_mp.bit_length() - 1
    place = lax.axis_index("dp") * n_mp + lax.axis_index("mp")
    rows = terms.shape[0] // (2 * n_mp)
    bits = list(range(top, -1, -1))
    values = terms.reshape((2,) * (top + 1) + (rows, terms.shape[1]))
    for bit in order:
        position = bits.index(bit)
        mine = place >> bit & 1
        keep = lax.dynamic_index_in_dim(values, mine, position, keepdims=False)
        send = lax.dynamic_index_in_dim(values, 1 - mine, position, keepdims=False)
        got = swap(send, "dp", 1) if bit == top else swap(send, "mp", 1 << bit)
        values = keep + got
        bits.pop(position)
    return values.reshape(rows, terms.shape[1])


def doubling_step(current, order, step):
    own = lax.axis_index("mp")
    bit = order[step]
    got = swap(current, "mp", 1 << bit)
    low = jnp.where(own >> bit & 1 == 0, current, got)
    high = jnp.where(own >> bit & 1 == 0, got, current)
    return jnp.stack([low, high], axis=sum((1 for done in order[:step] if done > bit)))


def doubling_gather(rows, order):
    current = rows
    for step in range(len(order)):
        current = doubling_step(current, order, step)
    return current.reshape(-1, rows.shape[-1])


def split_gather(rows, order, other):
    if other == order:
        return doubling_gather(rows, order)
    half = rows.shape[1] // 2
    return jnp.concatenate(
        [doubling_gather(rows[:, :half], order), doubling_gather(rows[:, half:], other)], axis=1
    )


def shards(
    node_features, weights_one, weights_two, neighbor_owner, neighbor_row, neighbor_count, cotangent
):
    devices = lax.axis_size("mp")
    own_index = lax.axis_index("mp")
    node_dev = cotangent.shape[0]
    all_nodes = neighbor_owner.shape[0]
    fanout = neighbor_owner.shape[1]
    feat_width = weights_one.shape[0] // 2
    hidden = weights_one.shape[1]
    live = lax.broadcasted_iota(jnp.int32, (all_nodes, fanout), 1) < neighbor_count[:, None]
    inverse_all = 1.0 / neighbor_count.astype(jnp.float32)
    owner_ids = lax.broadcasted_iota(jnp.int32, (devices, 1, 1), 0)
    match = (neighbor_owner[None, :, :] == owner_ids) & live[None, :, :]
    rowsel = jnp.max(jnp.where(match, neighbor_row[None, :, :], -1), axis=2)
    self_two = weights_two[:hidden]
    neigh_two = weights_two[hidden:]
    own_inverse = lax.dynamic_slice_in_dim(inverse_all, own_index * node_dev, node_dev, 0)
    order = list(range(devices.bit_length() - 2, -1, -1))
    other = [1] + [bit for bit in order if bit != 1] if devices == 16 else order
    dense_one = all_nodes * all_nodes <= 4096 * 4096
    down_neigh = (contract(cotangent, neigh_two, 1, 1) * own_inverse[:, None]).astype(jnp.bfloat16)
    half = down_neigh.shape[1] // 2
    parts = [down_neigh[:, :half], down_neigh[:, half:]]
    orders = [order, other]
    steps_done = 0

    def advance(parts, steps_done):
        if steps_done < len(order):
            parts = [doubling_step(p, o, steps_done) for p, o in zip(parts, orders)]
        return (parts, steps_done + 1)

    parts, steps_done = advance(parts, steps_done)
    with jax.named_scope("layer_one_mean"):
        if dense_one:
            row_ids = lax.broadcasted_iota(jnp.int32, (1, node_dev, 1), 1)
            adjacency = (rowsel[:, None, :] == row_ids).astype(jnp.bfloat16)
            adjacency = adjacency.reshape(devices * node_dev, all_nodes)
            parts, adjacency = lax.optimization_barrier((parts, adjacency))
            parts, steps_done = advance(parts, steps_done)
            summed = contract(node_features, adjacency, 1, 0)
            agg_one_cols = (summed * inverse_all[None, :]).astype(jnp.bfloat16)
        else:
            owner_slots = neighbor_owner.T
            global_ids = owner_slots * node_dev + neighbor_row.T
            agg_one_cols = column_mean(node_features, global_ids, live.T, inverse_all)
    parts, agg_one_cols = lax.optimization_barrier((parts, agg_one_cols))
    parts, steps_done = advance(parts, steps_done)
    own_feats, own_agg_one = (
        lax.all_to_all(node_features, "mp", split_axis=1, concat_axis=0, tiled=True),
        lax.all_to_all(agg_one_cols, "mp", split_axis=1, concat_axis=0, tiled=True),
    )
    parts, own_agg_one = lax.optimization_barrier((parts, own_agg_one))
    with jax.named_scope("neighbor_tables"):
        row_ids = lax.broadcasted_iota(jnp.int32, (1, node_dev, 1), 1)
        own_sel = lax.dynamic_slice_in_dim(rowsel, own_index * node_dev, node_dev, 1)
        own_edges = (own_sel[:, None, :] == row_ids).astype(jnp.bfloat16)
        own_edges = own_edges.reshape(devices * node_dev, node_dev)
        mine_sel = lax.dynamic_index_in_dim(rowsel, own_index, 0, keepdims=False)
        named_by = (mine_sel[:, None] == row_ids.reshape(1, node_dev)).astype(jnp.bfloat16)
    pre_one = contract(own_feats, weights_one[:feat_width], 0, 0) + contract(
        own_agg_one, weights_one[feat_width:], 0, 0
    )
    hidden_one = jax.nn.silu(pre_one).astype(jnp.bfloat16)
    hparts = [hidden_one[:, :half], hidden_one[:, half:]]
    hparts = [doubling_step(p, o, 0) for p, o in zip(hparts, orders)]
    hparts, parts = lax.optimization_barrier((hparts, parts))
    while steps_done < len(order):
        parts, steps_done = advance(parts, steps_done)
    for step in range(1, len(order)):
        hparts = [doubling_step(p, o, step) for p, o in zip(hparts, orders)]
    hidden_all = jnp.concatenate([p.reshape(-1, half) for p in hparts], axis=1)
    down_all = jnp.concatenate([p.reshape(-1, half) for p in parts], axis=1)
    total = contract(own_edges, hidden_all, 0, 0)
    agg_two = (total * own_inverse[:, None]).astype(jnp.bfloat16)
    node_output = (
        contract(hidden_one, self_two, 1, 0) + contract(agg_two, neigh_two, 1, 0)
    ).astype(jnp.bfloat16)
    down_self = contract(cotangent, self_two, 1, 1)
    neighbor_sum = contract(named_by, down_all, 0, 0)
    grad_hidden = down_self + neighbor_sum
    grad_pre = (grad_hidden * silu_slope(pre_one)).astype(jnp.bfloat16)
    terms = jnp.concatenate(
        [
            contract(own_feats, grad_pre, 1, 0),
            contract(own_agg_one, grad_pre, 1, 0),
            contract(hidden_one, cotangent, 0, 0),
            contract(agg_two, cotangent, 0, 0),
        ],
        axis=0,
    )
    with jax.named_scope("weight_grad_sum"):
        if lax.axis_size("dp") == 2 and devices == 16:
            half = terms.shape[1] // 2
            weight_grads = jnp.concatenate(
                [
                    halving_scatter(terms[:, :half], [0, 4, 1, 3, 2]),
                    halving_scatter(terms[:, half:], [0, 1, 4, 2, 3]),
                ],
                axis=1,
            )
        else:
            weight_grads = lax.psum_scatter(terms, ("dp", "mp"), scatter_dimension=0, tiled=True)
    return (node_output, weight_grads)


def solution(mesh):
    in_specs = (
        P("mp", "dp"),
        P(),
        P(),
        P("dp", None),
        P("dp", None),
        P("dp"),
        P(("dp", "mp"), None),
    )
    out_specs = (P(("dp", "mp"), None), P(("dp", "mp"), None))
    return jax.shard_map(shards, mesh=mesh, in_specs=in_specs, out_specs=out_specs, check_vma=False)
```

profile of v0, /device:TPU:0, one launch (start us, length us, event | category | flops | bytes accessed | tf_op | source)
XLA Modules:
  0.0 135.3 jit_solution(17648339066246796679)
XLA Ops:
  1.6 1.4 %fusion.21 = bf16[192,512]{1,0:T(8,128)(2,1)S(1)} fusion(bf16[192,512]{1,0:T(8,128)(2,1)S(1)} %copy-done, bf16[1024,512]{1,0:T(8,128)(2,1)} %param.9, f32[192]{0:T(256)S(1)} %dynamic_slice.78), kind=kOutput, calls=%fused_computation.33 | convolution fusion | flops 100859904 | bytes 918272 | tf_op jit(solution)/shard_map/dot_general | solution.py:22
  3.0 4.1 %collective-permute-start = (bf16[192,256]{1,0:T(8,128)(2,1)S(1)}, bf16[192,256]{1,0:T(8,128)(2,1)S(1)}, u32[]{:S(2)}, u32[]{:S(2)}) collective-permute-start(bf16[192,256]{1,0:T(8,128)(2,1)S(1)} %get-tuple-element.71), channel_id=1, source_target_pairs={{0,8},{1,9},{2,10},{3,11},{4,12},{5,13},{6,14},{7,15},{8,0},{9,1},... | collective-permute-start | bytes 294920 | tf_op jit(solution)/shard_map/ppermute | solution.py:29
  7.1 1.5 %collective-permute-start.1 = (bf16[192,256]{1,0:T(8,128)(2,1)S(1)}, bf16[192,256]{1,0:T(8,128)(2,1)S(1)}, u32[]{:S(2)}, u32[]{:S(2)}) collective-permute-start(bf16[192,256]{1,0:T(8,128)(2,1)S(1)} %get-tuple-element.70), channel_id=1, source_target_pairs={{0,2},{1,3},{2,0},{3,1},{4,6},{5,7},{6,4},{7,5},{8,10},{9,11},{10,... | collective-permute-start | bytes 294920 | tf_op jit(solution)/shard_map/ppermute | solution.py:29
  10.6 3.5 %all-to-all-start = ((bf16[32,16,192]{2,0,1:T(8,128)(2,1)}), bf16[32,16,192]{2,0,1:T(8,128)(2,1)S(1)}, u32[]{:S(2)}, u32[]{:S(2)}) async-start(bf16[32,16,192]{2,0,1:T(8,128)(2,1)} %copy.29), calls=%async_computation | async-start | bytes 524288 | tf_op jit(solution)/shard_map/all_to_all | solution.py:124
  15.2 3.9 %fusion = bf16[3072,3072]{1,0:T(8,128)(2,1)S(1)} fusion(s32[3072]{0:T(1024)S(1)} %eq.57, s32[16,3072]{1,0:T(8,128)S(1)} %select_reduce_fusion), kind=kLoop, calls=%fused_computation.1 | loop fusion | flops 18874368 | bytes 19083264 | tf_op jit(solution)/shard_map/layer_one_mean/convert_element_type | solution.py:111
  19.1 2.8 %collective-permute-start.3 = (bf16[2,192,256]{2,1,0:T(8,128)(2,1)S(1)}, bf16[2,192,256]{2,1,0:T(8,128)(2,1)S(1)}, u32[]{:S(2)}, u32[]{:S(2)}) collective-permute-start(bf16[2,192,256]{2,1,0:T(8,128)(2,1)S(1)} %get-tuple-element.16), channel_id=1, source_target_pairs={{0,8},{1,9},{2,10},{3,11},{4,12},{5,13},{6,14},{7,15},{8,0},{9,1},... | collective-permute-start | bytes 589832 | tf_op jit(solution)/shard_map/layer_one_mean/ppermute | solution.py:29
  22.0 1.5 %collective-permute-start.2 = (bf16[2,192,256]{2,1,0:T(8,128)(2,1)S(1)}, bf16[2,192,256]{2,1,0:T(8,128)(2,1)S(1)}, u32[]{:S(2)}, u32[]{:S(2)}) collective-permute-start(bf16[2,192,256]{2,1,0:T(8,128)(2,1)S(1)} %get-tuple-element.15), channel_id=1, source_target_pairs={{0,4},{1,5},{2,6},{3,7},{4,0},{5,1},{6,2},{7,3},{8,12},{9,13},{10,... | collective-permute-start | bytes 589832 | tf_op jit(solution)/shard_map/layer_one_mean/ppermute | solution.py:29
  23.4 3.4 %fusion.2 = bf16[32,3072]{1,0:T(8,128)(2,1)S(1)} fusion(bf16[32,3072]{1,0:T(8,128)(2,1)S(1)} %copy-done.3, bf16[3072,3072]{1,0:T(8,128)(2,1)S(1)} %fusion, f32[3072]{0:T(1024)S(1)} %convert_divide_fusion), kind=kOutput, calls=%fused_computation.5 | convolution fusion | flops 604176384 | bytes 19279872 | tf_op jit(solution)/shard_map/layer_one_mean/dot_general | solution.py:22
  26.8 5.5 %collective-permute-done.3 = bf16[2,192,256]{2,1,0:T(8,128)(2,1)S(1)} collective-permute-done((bf16[2,192,256]{2,1,0:T(8,128)(2,1)S(1)}, bf16[2,192,256]{2,1,0:T(8,128)(2,1)S(1)}, u32[]{:S(2)}, u32[]{:S(2)}) %collective-permute-start.3) | collective-permute-done | bytes 196640 | tf_op jit(solution)/shard_map/layer_one_mean/ppermute | solution.py:29
  33.4 1.5 %collective-permute-start.4 = (bf16[2,2,192,256]{3,2,0,1:T(8,128)(2,1)S(1)}, bf16[2,2,192,256]{3,2,0,1:T(8,128)(2,1)S(1)}, u32[]{:S(2)}, u32[]{:S(2)}) collective-permute-start(bf16[2,2,192,256]{3,2,0,1:T(8,128)(2,1)S(1)} %pad_maximum_fusion.9), channel_id=1, source_target_pairs={{0,2},{1,3},{2,0},{3,1},{4,6},{5,7},{6,4},{7,5},{8,10},{9,11},{10,... | collective-permute-start | bytes 1179656 | tf_op jit(solution)/shard_map/ppermute | solution.py:29
  35.9 3.8 %all-to-all-start.1 = ((bf16[32,16,192]{2,0,1:T(8,128)(2,1)}), bf16[32,16,192]{2,0,1:T(8,128)(2,1)S(1)}, u32[]{:S(2)}, u32[]{:S(2)}) async-start(bf16[32,16,192]{2,0,1:T(8,128)(2,1)} %copy.30), calls=%async_computation.1 | async-start | bytes 524288 | tf_op jit(solution)/shard_map/all_to_all | solution.py:125
  39.7 2.1 %fusion.24 = f32[192,512]{1,0:T(8,128)} fusion(bf16[512,192]{1,0:T(8,128)(2,1)S(1)} %bitcast.148, bf16[1024,512]{1,0:T(8,128)(2,1)} %param.8), kind=kOutput, calls=%fused_computation.56 | convolution fusion | flops 100663296 | bytes 1114112 | tf_op jit(solution)/shard_map/dot_general | solution.py:22
  41.8 1.6 %collective-permute-done.5 = bf16[2,2,192,256]{3,2,1,0:T(8,128)(2,1)S(1)} collective-permute-done((bf16[2,2,192,256]{3,2,1,0:T(8,128)(2,1)S(1)}, bf16[2,2,192,256]{3,2,1,0:T(8,128)(2,1)S(1)}, u32[]{:S(2)}, u32[]{:S(2)}) %collective-permute-start.5) | collective-permute-done | bytes 393248 | tf_op jit(solution)/shard_map/ppermute | solution.py:29
  43.9 5.8 %all-to-all-done.1 = bf16[32,16,192]{2,0,1:T(8,128)(2,1)S(1)} async-done(((bf16[32,16,192]{2,0,1:T(8,128)(2,1)}), bf16[32,16,192]{2,0,1:T(8,128)(2,1)S(1)}, u32[]{:S(2)}, u32[]{:S(2)}) %all-to-all-start.1) | async-done | bytes 196640 | tf_op jit(solution)/shard_map/all_to_all | solution.py:125
  49.7 2.1 %multiply_convert_fusion = (bf16[192,512]{1,0:T(8,128)(2,1)S(1)}, f32[192,512]{1,0:T(8,128)}) fusion(f32[192,512]{1,0:T(8,128)S(1)} %copy-done.9, bf16[512,192]{1,0:T(8,128)(2,1)S(1)} %bitcast.154, bf16[1024,512]{1,0:T(8,128)(2,1)} %param.8), kind=kOutput, calls=%fused_computation.71 | convolution fusion | flops 101253120 | bytes 1703936 | tf_op jit(solution)/shard_map/dot_general | solution.py:22
  53.0 1.4 %bitcast_compare_fusion.1 = pred[3072,192]{1,0:T(32,128)(4,1)} fusion(s32[3072]{0:T(1024)S(1)} %eq.57, s32[16,192]{1,0:T(8,128)S(1)} %constant_dynamic-slice_fusion.3), kind=kLoop, calls=%fused_computation.14 | loop fusion | flops 589824 | bytes 614400 | tf_op jit(solution)/shard_map/neighbor_tables/eq | solution.py:131
  54.4 5.0 %collective-permute-done.6 = bf16[192,256]{1,0:T(8,128)(2,1)S(1)} collective-permute-done((bf16[192,256]{1,0:T(8,128)(2,1)S(1)}, bf16[192,256]{1,0:T(8,128)(2,1)S(1)}, u32[]{:S(2)}, u32[]{:S(2)}) %collective-permute-start.6) | collective-permute-done | bytes 98336 | tf_op jit(solution)/shard_map/ppermute | solution.py:29
  59.7 2.1 %collective-permute-start.11 = (bf16[2,192,256]{2,1,0:T(8,128)(2,1)S(1)}, bf16[2,192,256]{2,1,0:T(8,128)(2,1)S(1)}, u32[]{:S(2)}, u32[]{:S(2)}) collective-permute-start(bf16[2,192,256]{2,1,0:T(8,128)(2,1)S(1)} %pad_maximum_fusion.16), channel_id=1, source_target_pairs={{0,8},{1,9},{2,10},{3,11},{4,12},{5,13},{6,14},{7,15},{8,0},{9,1},... | collective-permute-start | bytes 589832 | tf_op jit(solution)/shard_map/ppermute | solution.py:29
  61.9 6.8 %collective-permute-done.8 = bf16[2,192,256]{2,1,0:T(8,128)(2,1)S(1)} collective-permute-done((bf16[2,192,256]{2,1,0:T(8,128)(2,1)S(1)}, bf16[2,192,256]{2,1,0:T(8,128)(2,1)S(1)}, u32[]{:S(2)}, u32[]{:S(2)}) %collective-permute-start.8) | collective-permute-done | bytes 196640 | tf_op jit(solution)/shard_map/ppermute | solution.py:29
  69.9 2.3 %collective-permute-done.11 = bf16[2,192,256]{2,1,0:T(8,128)(2,1)S(1)} collective-permute-done((bf16[2,192,256]{2,1,0:T(8,128)(2,1)S(1)}, bf16[2,192,256]{2,1,0:T(8,128)(2,1)S(1)}, u32[]{:S(2)}, u32[]{:S(2)}) %collective-permute-start.11) | collective-permute-done | bytes 196640 | tf_op jit(solution)/shard_map/ppermute | solution.py:29
  72.8 5.9 %collective-permute-done.9 = bf16[2,2,192,256]{3,2,0,1:T(8,128)(2,1)S(1)} collective-permute-done((bf16[2,2,192,256]{3,2,0,1:T(8,128)(2,1)S(1)}, bf16[2,2,192,256]{3,2,0,1:T(8,128)(2,1)S(1)}, u32[]{:S(2)}, u32[]{:S(2)}) %collective-permute-start.9) | collective-permute-done | bytes 393248 | tf_op jit(solution)/shard_map/ppermute | solution.py:29
  78.9 4.1 %collective-permute-done.12 = bf16[2,2,192,256]{3,2,1,0:T(8,128)(2,1)S(1)} collective-permute-done((bf16[2,2,192,256]{3,2,1,0:T(8,128)(2,1)S(1)}, bf16[2,2,192,256]{3,2,1,0:T(8,128)(2,1)S(1)}, u32[]{:S(2)}, u32[]{:S(2)}) %collective-permute-start.12) | collective-permute-done | bytes 393248 | tf_op jit(solution)/shard_map/ppermute | solution.py:29
  84.1 1.6 %fusion.7 = f32[192,512]{1,0:T(8,128)S(1)} fusion(bf16[3072,256]{1,0:T(8,128)(2,1)S(1)} %bitcast.153, bf16[3072,256]{1,0:T(8,128)(2,1)S(1)} %bitcast.151, s32[3072]{0:T(1024)S(1)} %bitcast.156), kind=kOutput, calls=%fused_computation.10 | convolution fusion | flops 610861056 | bytes 3551232 | tf_op jit(solution)/shard_map/dot_general | solution.py:22
  97.8 1.6 %collective-permute-start.17 = (f32[2,2,2,64,256]{4,3,2,1,0:T(8,128)S(1)}, f32[2,2,2,64,256]{4,3,2,1,0:T(8,128)S(1)}, u32[]{:S(2)}, u32[]{:S(2)}) collective-permute-start(f32[2,2,2,64,256]{4,3,2,1,0:T(8,128)S(1)} %dynamic-slice_bitcast_fusion.2), channel_id=1, source_target_pairs={{0,16},{16,0},{1,17},{17,1},{2,18},{18,2},{3,19},{19,3},{4,20},{20... | collective-permute-start | bytes 1572872 | tf_op jit(solution)/shard_map/weight_grad_sum/ppermute | solution.py:29
  99.3 1.5 %bitcast_add_fusion = f32[2,2,2,2,64,256]{5,4,2,1,0,3:T(8,128)S(1)} fusion(f32[2,2,2,2,64,256]{5,4,2,1,0,3:T(8,128)} %collective-permute-done.21, f32[2,2,2,2,1,64,256]{6,5,4,3,2,1,0:T(8,128)S(1)} %get-tuple-element.30), kind=kLoop, calls=%fused_computation.35 | loop fusion | flops 262144 | bytes 3145728 | tf_op jit(solution)/shard_map/weight_grad_sum/add | solution.py:45
  102.1 9.9 %collective-permute-done.17 = f32[2,2,2,64,256]{4,3,2,1,0:T(8,128)S(1)} collective-permute-done((f32[2,2,2,64,256]{4,3,2,1,0:T(8,128)S(1)}, f32[2,2,2,64,256]{4,3,2,1,0:T(8,128)S(1)}, u32[]{:S(2)}, u32[]{:S(2)}) %collective-permute-start.17) | collective-permute-done | bytes 524320 | tf_op jit(solution)/shard_map/weight_grad_sum/ppermute | solution.py:29
  112.5 2.7 %collective-permute-done.22 = f32[2,2,2,64,256]{4,3,2,1,0:T(8,128)S(1)} collective-permute-done((f32[2,2,2,64,256]{4,3,2,1,0:T(8,128)S(1)}, f32[2,2,2,64,256]{4,3,2,1,0:T(8,128)S(1)}, u32[]{:S(2)}, u32[]{:S(2)}) %collective-permute-start.22) | collective-permute-done | bytes 524320 | tf_op jit(solution)/shard_map/weight_grad_sum/ppermute | solution.py:29
  115.6 4.9 %collective-permute-done.18 = f32[2,2,64,256]{3,2,1,0:T(8,128)S(1)} collective-permute-done((f32[2,2,64,256]{3,2,1,0:T(8,128)S(1)}, f32[2,2,64,256]{3,2,1,0:T(8,128)S(1)}, u32[]{:S(2)}, u32[]{:S(2)}) %collective-permute-start.18) | collective-permute-done | bytes 262176 | tf_op jit(solution)/shard_map/weight_grad_sum/ppermute | solution.py:29
  123.2 5.5 %collective-permute-done.19 = f32[2,64,256]{2,1,0:T(8,128)S(1)} collective-permute-done((f32[2,64,256]{2,1,0:T(8,128)S(1)}, f32[2,64,256]{2,1,0:T(8,128)S(1)}, u32[]{:S(2)}, u32[]{:S(2)}) %collective-permute-start.19) | collective-permute-done | bytes 131104 | tf_op jit(solution)/shard_map/weight_grad_sum/ppermute | solution.py:29
  129.4 1.9 %collective-permute-start.25 = (f32[64,256]{1,0:T(8,128)S(1)}, f32[64,256]{1,0:T(8,128)S(1)}, u32[]{:S(2)}, u32[]{:S(2)}) collective-permute-start(f32[64,256]{1,0:T(8,128)S(1)} %dynamic-slice_bitcast_fusion.7), channel_id=1, source_target_pairs={{0,8},{1,9},{2,10},{3,11},{4,12},{5,13},{6,14},{7,15},{8,0},{9,1},... | collective-permute-start | bytes 196616 | tf_op jit(solution)/shard_map/weight_grad_sum/ppermute | solution.py:29
  131.2 2.0 %collective-permute-done.20 = f32[64,256]{1,0:T(8,128)S(1)} collective-permute-done((f32[64,256]{1,0:T(8,128)S(1)}, f32[64,256]{1,0:T(8,128)S(1)}, u32[]{:S(2)}, u32[]{:S(2)}) %collective-permute-start.20) | collective-permute-done | bytes 65568 | tf_op jit(solution)/shard_map/weight_grad_sum/ppermute | solution.py:29
  133.3 1.4 %collective-permute-done.25 = f32[64,256]{1,0:T(8,128)S(1)} collective-permute-done((f32[64,256]{1,0:T(8,128)S(1)}, f32[64,256]{1,0:T(8,128)S(1)}, u32[]{:S(2)}, u32[]{:S(2)}) %collective-permute-start.25) | collective-permute-done | bytes 65568 | tf_op jit(solution)/shard_map/weight_grad_sum/ppermute | solution.py:29
  (138 shorter events, 29.1 us)
Async XLA Ops:
  0.6 13.5 %copy-start.12 = (s32[3072]{0:T(1024)S(1)}, s32[3072]{0:T(1024)}, u32[]{:S(2)}) copy-start(s32[3072]{0:T(1024)} %param.12) | copy-start | bytes 36868
  0.7 13.6 %copy-start.11 = (s32[3072,8]{0,1:T(8,128)S(1)}, s32[3072,8]{0,1:T(8,128)}, u32[]{:S(2)}) copy-start(s32[3072,8]{0,1:T(8,128)} %param.10) | copy-start | bytes 294916
  0.7 13.6 %copy-start.10 = (s32[3072,8]{0,1:T(8,128)S(1)}, s32[3072,8]{0,1:T(8,128)}, u32[]{:S(2)}) copy-start(s32[3072,8]{0,1:T(8,128)} %param.11) | copy-start | bytes 294916
  3.0 16.1 %collective-permute-start = (bf16[192,256]{1,0:T(8,128)(2,1)S(1)}, bf16[192,256]{1,0:T(8,128)(2,1)S(1)}, u32[]{:S(2)}, u32[]{:S(2)}) collective-permute-start(bf16[192,256]{1,0:T(8,128)(2,1)S(1)} %get-tuple-element.71), channel_id=1, source_target_pairs={{0,8},{1,9},{2,10},{3,11},{4,12},{5,13},{6,14},{7,15},{8,0},{9,1},... | collective-permute-start | bytes 294920 | tf_op jit(solution)/shard_map/ppermute | solution.py:29
  7.1 12.0 %collective-permute-start.1 = (bf16[192,256]{1,0:T(8,128)(2,1)S(1)}, bf16[192,256]{1,0:T(8,128)(2,1)S(1)}, u32[]{:S(2)}, u32[]{:S(2)}) collective-permute-start(bf16[192,256]{1,0:T(8,128)(2,1)S(1)} %get-tuple-element.70), channel_id=1, source_target_pairs={{0,2},{1,3},{2,0},{3,1},{4,6},{5,7},{6,4},{7,5},{8,10},{9,11},{10,... | collective-permute-start | bytes 294920 | tf_op jit(solution)/shard_map/ppermute | solution.py:29
  10.6 25.3 %all-to-all-start = ((bf16[32,16,192]{2,0,1:T(8,128)(2,1)}), bf16[32,16,192]{2,0,1:T(8,128)(2,1)S(1)}, u32[]{:S(2)}, u32[]{:S(2)}) async-start(bf16[32,16,192]{2,0,1:T(8,128)(2,1)} %copy.29), calls=%async_computation | async-start | bytes 524288 | tf_op jit(solution)/shard_map/all_to_all | solution.py:124
  15.1 8.3 %copy-start.3 = (bf16[32,3072]{1,0:T(8,128)(2,1)S(1)}, bf16[32,3072]{1,0:T(8,128)(2,1)}, u32[]{:S(2)}) copy-start(bf16[32,3072]{1,0:T(8,128)(2,1)} %param.7) | copy-start | bytes 589828
  19.1 13.1 %collective-permute-start.3 = (bf16[2,192,256]{2,1,0:T(8,128)(2,1)S(1)}, bf16[2,192,256]{2,1,0:T(8,128)(2,1)S(1)}, u32[]{:S(2)}, u32[]{:S(2)}) collective-permute-start(bf16[2,192,256]{2,1,0:T(8,128)(2,1)S(1)} %get-tuple-element.16), channel_id=1, source_target_pairs={{0,8},{1,9},{2,10},{3,11},{4,12},{5,13},{6,14},{7,15},{8,0},{9,1},... | collective-permute-start | bytes 589832 | tf_op jit(solution)/shard_map/layer_one_mean/ppermute | solution.py:29
  22.0 10.4 %collective-permute-start.2 = (bf16[2,192,256]{2,1,0:T(8,128)(2,1)S(1)}, bf16[2,192,256]{2,1,0:T(8,128)(2,1)S(1)}, u32[]{:S(2)}, u32[]{:S(2)}) collective-permute-start(bf16[2,192,256]{2,1,0:T(8,128)(2,1)S(1)} %get-tuple-element.15), channel_id=1, source_target_pairs={{0,4},{1,5},{2,6},{3,7},{4,0},{5,1},{6,2},{7,3},{8,12},{9,13},{10,... | collective-permute-start | bytes 589832 | tf_op jit(solution)/shard_map/layer_one_mean/ppermute | solution.py:29
  32.5 10.8 %collective-permute-start.5 = (bf16[2,2,192,256]{3,2,1,0:T(8,128)(2,1)S(1)}, bf16[2,2,192,256]{3,2,1,0:T(8,128)(2,1)S(1)}, u32[]{:S(2)}, u32[]{:S(2)}) collective-permute-start(bf16[2,2,192,256]{3,2,1,0:T(8,128)(2,1)S(1)} %pad_maximum_fusion.10), channel_id=1, source_target_pairs={{0,4},{1,5},{2,6},{3,7},{4,0},{5,1},{6,2},{7,3},{8,12},{9,13},{10,... | collective-permute-start | bytes 1179656 | tf_op jit(solution)/shard_map/ppermute | solution.py:29
  33.4 10.4 %collective-permute-start.4 = (bf16[2,2,192,256]{3,2,0,1:T(8,128)(2,1)S(1)}, bf16[2,2,192,256]{3,2,0,1:T(8,128)(2,1)S(1)}, u32[]{:S(2)}, u32[]{:S(2)}) collective-permute-start(bf16[2,2,192,256]{3,2,0,1:T(8,128)(2,1)S(1)} %pad_maximum_fusion.9), channel_id=1, source_target_pairs={{0,2},{1,3},{2,0},{3,1},{4,6},{5,7},{6,4},{7,5},{8,10},{9,11},{10,... | collective-permute-start | bytes 1179656 | tf_op jit(solution)/shard_map/ppermute | solution.py:29
  35.9 13.8 %all-to-all-start.1 = ((bf16[32,16,192]{2,0,1:T(8,128)(2,1)}), bf16[32,16,192]{2,0,1:T(8,128)(2,1)S(1)}, u32[]{:S(2)}, u32[]{:S(2)}) async-start(bf16[32,16,192]{2,0,1:T(8,128)(2,1)} %copy.30), calls=%async_computation.1 | async-start | bytes 524288 | tf_op jit(solution)/shard_map/all_to_all | solution.py:125
  51.8 7.6 %collective-permute-start.6 = (bf16[192,256]{1,0:T(8,128)(2,1)S(1)}, bf16[192,256]{1,0:T(8,128)(2,1)S(1)}, u32[]{:S(2)}, u32[]{:S(2)}) collective-permute-start(bf16[192,256]{1,0:T(8,128)(2,1)S(1)} %get-tuple-element.67), channel_id=1, source_target_pairs={{0,8},{1,9},{2,10},{3,11},{4,12},{5,13},{6,14},{7,15},{8,0},{9,1},... | collective-permute-start | bytes 294920 | tf_op jit(solution)/shard_map/ppermute | solution.py:29
  53.0 6.5 %collective-permute-start.7 = (bf16[192,256]{1,0:T(8,128)(2,1)S(1)}, bf16[192,256]{1,0:T(8,128)(2,1)S(1)}, u32[]{:S(2)}, u32[]{:S(2)}) collective-permute-start(bf16[192,256]{1,0:T(8,128)(2,1)S(1)} %get-tuple-element.66), channel_id=1, source_target_pairs={{0,2},{1,3},{2,0},{3,1},{4,6},{5,7},{6,4},{7,5},{8,10},{9,11},{10,... | collective-permute-start | bytes 294920 | tf_op jit(solution)/shard_map/ppermute | solution.py:29
  59.6 9.1 %collective-permute-start.8 = (bf16[2,192,256]{2,1,0:T(8,128)(2,1)S(1)}, bf16[2,192,256]{2,1,0:T(8,128)(2,1)S(1)}, u32[]{:S(2)}, u32[]{:S(2)}) collective-permute-start(bf16[2,192,256]{2,1,0:T(8,128)(2,1)S(1)} %pad_maximum_fusion.15), channel_id=1, source_target_pairs={{0,4},{1,5},{2,6},{3,7},{4,0},{5,1},{6,2},{7,3},{8,12},{9,13},{10,... | collective-permute-start | bytes 589832 | tf_op jit(solution)/shard_map/ppermute | solution.py:29
  59.7 23.6 %collective-permute-start.14 = (bf16[2,2,2,192,256]{4,3,0,1,2:T(8,128)(2,1)S(1)}, bf16[2,2,2,192,256]{4,3,0,1,2:T(8,128)(2,1)S(1)}, u32[]{:S(2)}, u32[]{:S(2)}) collective-permute-start(bf16[2,2,2,192,256]{4,3,0,1,2:T(8,128)(2,1)S(1)} %pad_maximum_fusion.5), channel_id=1, source_target_pairs={{0,1},{1,0},{2,3},{3,2},{4,5},{5,4},{6,7},{7,6},{8,9},{9,8},{10,11... | collective-permute-start | bytes 2359304 | tf_op jit(solution)/shard_map/ppermute | solution.py:29
  59.7 12.5 %collective-permute-start.11 = (bf16[2,192,256]{2,1,0:T(8,128)(2,1)S(1)}, bf16[2,192,256]{2,1,0:T(8,128)(2,1)S(1)}, u32[]{:S(2)}, u32[]{:S(2)}) collective-permute-start(bf16[2,192,256]{2,1,0:T(8,128)(2,1)S(1)} %pad_maximum_fusion.16), channel_id=1, source_target_pairs={{0,8},{1,9},{2,10},{3,11},{4,12},{5,13},{6,14},{7,15},{8,0},{9,1},... | collective-permute-start | bytes 589832 | tf_op jit(solution)/shard_map/ppermute | solution.py:29
  68.8 9.9 %collective-permute-start.9 = (bf16[2,2,192,256]{3,2,0,1:T(8,128)(2,1)S(1)}, bf16[2,2,192,256]{3,2,0,1:T(8,128)(2,1)S(1)}, u32[]{:S(2)}, u32[]{:S(2)}) collective-permute-start(bf16[2,2,192,256]{3,2,0,1:T(8,128)(2,1)S(1)} %pad_maximum_fusion.11), channel_id=1, source_target_pairs={{0,2},{1,3},{2,0},{3,1},{4,6},{5,7},{6,4},{7,5},{8,10},{9,11},{10,... | collective-permute-start | bytes 1179656 | tf_op jit(solution)/shard_map/ppermute | solution.py:29
  72.3 10.7 %collective-permute-start.12 = (bf16[2,2,192,256]{3,2,1,0:T(8,128)(2,1)S(1)}, bf16[2,2,192,256]{3,2,1,0:T(8,128)(2,1)S(1)}, u32[]{:S(2)}, u32[]{:S(2)}) collective-permute-start(bf16[2,2,192,256]{3,2,1,0:T(8,128)(2,1)S(1)} %pad_maximum_fusion.12), channel_id=1, source_target_pairs={{0,4},{1,5},{2,6},{3,7},{4,0},{5,1},{6,2},{7,3},{8,12},{9,13},{10,... | collective-permute-start | bytes 1179656 | tf_op jit(solution)/shard_map/ppermute | solution.py:29
  72.7 11.0 %collective-permute-start.15 = (bf16[2,2,2,192,256]{4,3,2,0,1:T(8,128)(2,1)S(1)}, bf16[2,2,2,192,256]{4,3,2,0,1:T(8,128)(2,1)S(1)}, u32[]{:S(2)}, u32[]{:S(2)}) collective-permute-start(bf16[2,2,2,192,256]{4,3,2,0,1:T(8,128)(2,1)S(1)} %pad_maximum_fusion.6), channel_id=1, source_target_pairs={{0,1},{1,0},{2,3},{3,2},{4,5},{5,4},{6,7},{7,6},{8,9},{9,8},{10,11... | collective-permute-start | bytes 2359304 | tf_op jit(solution)/shard_map/ppermute | solution.py:29
  78.8 7.8 %collective-permute-start.10 = (bf16[2,2,2,192,256]{4,3,0,1,2:T(8,128)(2,1)S(1)}, bf16[2,2,2,192,256]{4,3,0,1,2:T(8,128)(2,1)S(1)}, u32[]{:S(2)}, u32[]{:S(2)}) collective-permute-start(bf16[2,2,2,192,256]{4,3,0,1,2:T(8,128)(2,1)S(1)} %pad_maximum_fusion.7), channel_id=1, source_target_pairs={{0,1},{1,0},{2,3},{3,2},{4,5},{5,4},{6,7},{7,6},{8,9},{9,8},{10,11... | collective-permute-start | bytes 2359304 | tf_op jit(solution)/shard_map/ppermute | solution.py:29
  83.2 3.9 %collective-permute-start.13 = (bf16[2,2,2,192,256]{4,3,2,0,1:T(8,128)(2,1)S(1)}, bf16[2,2,2,192,256]{4,3,2,0,1:T(8,128)(2,1)S(1)}, u32[]{:S(2)}, u32[]{:S(2)}) collective-permute-start(bf16[2,2,2,192,256]{4,3,2,0,1:T(8,128)(2,1)S(1)} %pad_maximum_fusion.8), channel_id=1, source_target_pairs={{0,1},{1,0},{2,3},{3,2},{4,5},{5,4},{6,7},{7,6},{8,9},{9,8},{10,11... | collective-permute-start | bytes 2359304 | tf_op jit(solution)/shard_map/ppermute | solution.py:29
  93.2 3.1 %collective-permute-start.16 = (f32[2,2,2,2,64,256]{5,4,3,2,1,0:T(8,128)}, f32[2,2,2,2,64,256]{5,4,3,2,1,0:T(8,128)}, u32[]{:S(2)}, u32[]{:S(2)}) collective-permute-start(f32[2,2,2,2,64,256]{5,4,3,2,1,0:T(8,128)} %dynamic-slice_bitcast_fusion), channel_id=1, source_target_pairs={{0,1},{1,0},{2,3},{3,2},{4,5},{5,4},{6,7},{7,6},{8,9},{9,8},{10,11... | collective-permute-start | bytes 3145736 | tf_op jit(solution)/shard_map/weight_grad_sum/ppermute | solution.py:29
  94.9 4.4 %collective-permute-start.21 = (f32[2,2,2,2,64,256]{5,4,2,1,0,3:T(8,128)}, f32[2,2,2,2,64,256]{5,4,2,1,0,3:T(8,128)}, u32[]{:S(2)}, u32[]{:S(2)}) collective-permute-start(f32[2,2,2,2,64,256]{5,4,2,1,0,3:T(8,128)} %bitcast.144), channel_id=1, source_target_pairs={{0,1},{1,0},{2,3},{3,2},{4,5},{5,4},{6,7},{7,6},{8,9},{9,8},{10,11... | collective-permute-start | bytes 3145736 | tf_op jit(solution)/shard_map/weight_grad_sum/ppermute | solution.py:29
  97.8 14.3 %collective-permute-start.17 = (f32[2,2,2,64,256]{4,3,2,1,0:T(8,128)S(1)}, f32[2,2,2,64,256]{4,3,2,1,0:T(8,128)S(1)}, u32[]{:S(2)}, u32[]{:S(2)}) collective-permute-start(f32[2,2,2,64,256]{4,3,2,1,0:T(8,128)S(1)} %dynamic-slice_bitcast_fusion.2), channel_id=1, source_target_pairs={{0,16},{16,0},{1,17},{17,1},{2,18},{18,2},{3,19},{19,3},{4,20},{20... | collective-permute-start | bytes 1572872 | tf_op jit(solution)/shard_map/weight_grad_sum/ppermute | solution.py:29
  100.8 14.4 %collective-permute-start.22 = (f32[2,2,2,64,256]{4,3,2,1,0:T(8,128)S(1)}, f32[2,2,2,64,256]{4,3,2,1,0:T(8,128)S(1)}, u32[]{:S(2)}, u32[]{:S(2)}) collective-permute-start(f32[2,2,2,64,256]{4,3,2,1,0:T(8,128)S(1)} %dynamic-slice_bitcast_fusion.1), channel_id=1, source_target_pairs={{0,2},{1,3},{2,0},{3,1},{4,6},{5,7},{6,4},{7,5},{8,10},{9,11},{10,... | collective-permute-start | bytes 1572872 | tf_op jit(solution)/shard_map/weight_grad_sum/ppermute | solution.py:29
  112.2 8.3 %collective-permute-start.18 = (f32[2,2,64,256]{3,2,1,0:T(8,128)S(1)}, f32[2,2,64,256]{3,2,1,0:T(8,128)S(1)}, u32[]{:S(2)}, u32[]{:S(2)}) collective-permute-start(f32[2,2,64,256]{3,2,1,0:T(8,128)S(1)} %dynamic-slice_bitcast_fusion.4), channel_id=1, source_target_pairs={{0,2},{1,3},{2,0},{3,1},{4,6},{5,7},{6,4},{7,5},{8,10},{9,11},{10,... | collective-permute-start | bytes 786440 | tf_op jit(solution)/shard_map/weight_grad_sum/ppermute | solution.py:29
  115.3 7.3 %collective-permute-start.23 = (f32[2,2,64,256]{3,2,1,0:T(8,128)S(1)}, f32[2,2,64,256]{3,2,1,0:T(8,128)S(1)}, u32[]{:S(2)}, u32[]{:S(2)}) collective-permute-start(f32[2,2,64,256]{3,2,1,0:T(8,128)S(1)} %dynamic-slice_bitcast_fusion.3), channel_id=1, source_target_pairs={{0,16},{16,0},{1,17},{17,1},{2,18},{18,2},{3,19},{19,3},{4,20},{20... | collective-permute-start | bytes 786440 | tf_op jit(solution)/shard_map/weight_grad_sum/ppermute | solution.py:29
  120.6 8.1 %collective-permute-start.19 = (f32[2,64,256]{2,1,0:T(8,128)S(1)}, f32[2,64,256]{2,1,0:T(8,128)S(1)}, u32[]{:S(2)}, u32[]{:S(2)}) collective-permute-start(f32[2,64,256]{2,1,0:T(8,128)S(1)} %dynamic-slice_bitcast_fusion.6), channel_id=1, source_target_pairs={{0,8},{1,9},{2,10},{3,11},{4,12},{5,13},{6,14},{7,15},{8,0},{9,1},... | collective-permute-start | bytes 393224 | tf_op jit(solution)/shard_map/weight_grad_sum/ppermute | solution.py:29
  122.7 6.7 %collective-permute-start.24 = (f32[2,64,256]{2,1,0:T(8,128)S(1)}, f32[2,64,256]{2,1,0:T(8,128)S(1)}, u32[]{:S(2)}, u32[]{:S(2)}) collective-permute-start(f32[2,64,256]{2,1,0:T(8,128)S(1)} %dynamic-slice_bitcast_fusion.5), channel_id=1, source_target_pairs={{0,4},{1,5},{2,6},{3,7},{4,0},{5,1},{6,2},{7,3},{8,12},{9,13},{10,... | collective-permute-start | bytes 393224 | tf_op jit(solution)/shard_map/weight_grad_sum/ppermute | solution.py:29
  128.7 4.5 %collective-permute-start.20 = (f32[64,256]{1,0:T(8,128)S(1)}, f32[64,256]{1,0:T(8,128)S(1)}, u32[]{:S(2)}, u32[]{:S(2)}) collective-permute-start(f32[64,256]{1,0:T(8,128)S(1)} %dynamic-slice_bitcast_fusion.8), channel_id=1, source_target_pairs={{0,4},{1,5},{2,6},{3,7},{4,0},{5,1},{6,2},{7,3},{8,12},{9,13},{10,... | collective-permute-start | bytes 196616 | tf_op jit(solution)/shard_map/weight_grad_sum/ppermute | solution.py:29
  129.4 5.2 %collective-permute-start.25 = (f32[64,256]{1,0:T(8,128)S(1)}, f32[64,256]{1,0:T(8,128)S(1)}, u32[]{:S(2)}, u32[]{:S(2)}) collective-permute-start(f32[64,256]{1,0:T(8,128)S(1)} %dynamic-slice_bitcast_fusion.7), channel_id=1, source_target_pairs={{0,8},{1,9},{2,10},{3,11},{4,12},{5,13},{6,14},{7,15},{8,0},{9,1},... | collective-permute-start | bytes 196616 | tf_op jit(solution)/shard_map/weight_grad_sum/ppermute | solution.py:29
  (10 other events, 20.0 us)
where the time goes:
time: 136 us; the launch traced here: 135 us
  waiting for transfers between devices  65.7 us (48%)
  starting transfers between devices  30.6 us (22%)
  matrix products  15.4 us (11%)
  other arithmetic  13.1 us (10%)
  local copies, waits for them, and re-layouts  9.17 us (7%)
  between operations  1.38 us (1%)
    ppermute x26, waiting for transfers between devices, swap(): return lax.ppermute(values, axis, [(j, j ^ mask) for j in range(size)])  59.9 us
    ppermute x26, starting transfers between devices, swap(): return lax.ppermute(values, axis, [(j, j ^ mask) for j in range(size)])  23.3 us
    dot_general x13, matrix products, contract(): lax.dot_general(left, right, (((left_dim,), (right_dim,)), ((), ())), pre...  15.4 us
    all_to_all x1, waiting for transfers between devices, shards(): lax.all_to_all(agg_one_cols, 'mp', split_axis=1, concat_axis=0, tiled=True)  5.82 us
    convert_element_type x1, other arithmetic, shards(): adjacency = (rowsel[:, None, :] == row_ids).astype(jnp.bfloat16)  3.87 us
    all_to_all x1, starting transfers between devices, shards(): lax.all_to_all(agg_one_cols, 'mp', split_axis=1, concat_axis=0, tiled=True)  3.77 us
    all_to_all x1, starting transfers between devices, shards(): lax.all_to_all(node_features, 'mp', split_axis=1, concat_axis=0, tiled=True)  3.53 us
    add x10, other arithmetic, halving_scatter(): values = keep + got  3.09 us
  transfers between devices with their start and end apart: 28, of which 19 were waited for; matrix products, arithmetic and copies ran while one was open for 18% of the time, Pallas kernels for 0%

commit v1 on v0

--- a/solution.py
+++ b/solution.py
@@ -2,6 +2,22 @@
 import jax.numpy as jnp
 from jax import lax
 from jax.sharding import PartitionSpec as P
+
+
+def swapped_with_each(x, axis, split, join):
+    ways, here = (lax.axis_size(axis), lax.axis_index(axis))
+    width = x.shape[split] // ways
+    shape = list(x.shape)
+    shape[split] = width
+    height = shape[join]
+    shape[join] = height * ways
+    full = jnp.zeros(shape, x.dtype)
+    for mask in range(ways):
+        part = lax.dynamic_slice_in_dim(x, (here ^ mask) * width, width, axis=split)
+        if mask:
+            part = lax.ppermute(part, axis, [(d, d ^ mask) for d in range(ways)])
+        full = lax.dynamic_update_slice_in_dim(full, part, (here ^ mask) * height, axis=join)
+    return full
 
 
 def column_mean(table, indices, live, inverse):
@@ -122,7 +138,7 @@
     parts, steps_done = advance(parts, steps_done)
     own_feats, own_agg_one = (
         lax.all_to_all(node_features, "mp", split_axis=1, concat_axis=0, tiled=True),
-        lax.all_to_all(agg_one_cols, "mp", split_axis=1, concat_axis=0, tiled=True),
+        swapped_with_each(agg_one_cols, "mp", 1, 0),
     )
     parts, own_agg_one = lax.optimization_barrier((parts, own_agg_one))
     with jax.named_scope("neighbor_tables"):

time: 136 us -> 156 us (1.15)
  starting transfers between devices: 30.6 us -> 53.1 us
  waiting for transfers between devices: 65.7 us -> 54.4 us
  other arithmetic: 13.1 us -> 18.1 us
  matrix products: 15.4 us -> 20 us
    ppermute x0 -> x15, starting transfers between devices: none -> 21.6 us  [swapped_with_each(): part = lax.ppermute(part, axis, [(d, d ^ mask) for d in range(ways)])]
    ppermute x26, waiting for transfers between devices: 59.9 us -> 50.9 us  [swap(): return lax.ppermute(values, axis, [(j, j ^ mask) for j in range(size)])]
    all_to_all x1 -> x0, waiting for transfers between devices: 5.82 us -> none  [shards(): lax.all_to_all(agg_one_cols, 'mp', split_axis=1, concat_axis=0, tiled=True)]
    dot_general x13, matrix products: 15.4 us -> 20 us  [contract(): lax.dot_general(left, right, (((left_dim,), (right_dim,)), ((), ())), pre...]
    ppermute x26, starting transfers between devices: 23.3 us -> 27.5 us  [swap(): return lax.ppermute(values, axis, [(j, j ^ mask) for j in range(size)])]
    all_to_all x1 -> x0, starting transfers between devices: 3.77 us -> none  [shards(): lax.all_to_all(agg_one_cols, 'mp', split_axis=1, concat_axis=0, tiled=True)]
    ppermute x0 -> x15, waiting for transfers between devices: none -> 3.45 us  [swapped_with_each(): part = lax.ppermute(part, axis, [(d, d ^ mask) for d in range(ways)])]
    convert_element_type x1, other arithmetic: 3.87 us -> 7.25 us  [shards(): adjacency = (rowsel[:, None, :] == row_ids).astype(jnp.bfloat16)]
  transfers between devices with their start and end apart: 28 -> 42, of which waited for: 19 -> 16; matrix products, arithmetic and copies ran while one was open for 18% -> 22% of each run, Pallas kernels for 0% -> 0%
where the time goes in v1:
time: 156 us
  waiting for transfers between devices  54.4 us (35%)
  starting transfers between devices  53.1 us (34%)
  matrix products  20 us (13%)
  other arithmetic  18.1 us (12%)
  local copies, waits for them, and re-layouts  8.43 us (5%)
  between operations  1.6 us (1%)
    ppermute x26, waiting for transfers between devices, swap(): return lax.ppermute(values, axis, [(j, j ^ mask) for j in range(size)])  50.9 us
    ppermute x26, starting transfers between devices, swap(): return lax.ppermute(values, axis, [(j, j ^ mask) for j in range(size)])  27.5 us
    ppermute x15, starting transfers between devices, swapped_with_each(): part = lax.ppermute(part, axis, [(d, d ^ mask) for d in range(ways)])  21.6 us
    dot_general x13, matrix products, contract(): lax.dot_general(left, right, (((left_dim,), (right_dim,)), ((), ())), pre...  20 us
    convert_element_type x1, other arithmetic, shards(): adjacency = (rowsel[:, None, :] == row_ids).astype(jnp.bfloat16)  7.25 us
    all_to_all x1, starting transfers between devices, shards(): lax.all_to_all(node_features, 'mp', split_axis=1, concat_axis=0, tiled=True)  4.08 us
    unnamed x22, local copies, waits for them, and re-layouts  3.45 us
    ppermute x15, waiting for transfers between devices, swapped_with_each(): part = lax.ppermute(part, axis, [(d, d ^ mask) for d in range(ways)])  3.45 us
  transfers between devices with their start and end apart: 42, of which 16 were waited for; matrix products, arithmetic and copies ran while one was open for 22% of the time, Pallas kernels for 0%

profile of v1, /device:TPU:0, one launch (start us, length us, event | category | flops | bytes accessed | tf_op | source)
XLA Modules:
  0.0 155.6 jit_solution(16105057386942671410)
XLA Ops:
  3.0 4.1 %collective-permute-start = (bf16[192,256]{1,0:T(8,128)(2,1)S(1)}, bf16[192,256]{1,0:T(8,128)(2,1)S(1)}, u32[]{:S(2)}, u32[]{:S(2)}) collective-permute-start(bf16[192,256]{1,0:T(8,128)(2,1)S(1)} %get-tuple-element.87), channel_id=1, source_target_pairs={{0,8},{1,9},{2,10},{3,11},{4,12},{5,13},{6,14},{7,15},{8,0},{9,1},... | collective-permute-start | bytes 294920 | tf_op jit(solution)/shard_map/ppermute | solution.py:45
  7.1 1.5 collective-permute-start.1
  9.5 1.8 %select_reduce_fusion = s32[16,3072]{1,0:T(8,128)S(1)} fusion(s32[3072,8]{0,1:T(8,128)} %param.11, s32[3072,8]{0,1:T(8,128)} %param.10, pred[3072,8]{0,1:T(8,128)(4,1)S(1)} %iota_compare_fusion.3), kind=kLoop, calls=%fused_computation.21 | loop fusion | flops 1523712 | bytes 417792 | tf_op jit(solution)/shard_map/reduce_max | solution.py:105
  11.3 7.3 %fusion = bf16[3072,3072]{1,0:T(8,128)(2,1)} fusion(s32[3072]{0:T(1024)S(1)} %eq.57, s32[16,3072]{1,0:T(8,128)S(1)} %select_reduce_fusion), kind=kLoop, calls=%fused_computation.1 | loop fusion | flops 18874368 | bytes 19083264 | tf_op jit(solution)/shard_map/layer_one_mean/convert_element_type | solution.py:127
  19.0 1.6 %collective-permute-start.2 = (bf16[2,192,256]{2,1,0:T(8,128)(2,1)S(1)}, bf16[2,192,256]{2,1,0:T(8,128)(2,1)S(1)}, u32[]{:S(2)}, u32[]{:S(2)}) collective-permute-start(bf16[2,192,256]{2,1,0:T(8,128)(2,1)S(1)} %get-tuple-element.15), channel_id=1, source_target_pairs={{0,4},{1,5},{2,6},{3,7},{4,0},{5,1},{6,2},{7,3},{8,12},{9,13},{10,... | collective-permute-start | bytes 589832 | tf_op jit(solution)/shard_map/layer_one_mean/ppermute | solution.py:45
  20.6 9.7 %fusion.2 = bf16[32,3072]{1,0:T(8,128)(2,1)S(1)} fusion(bf16[32,3072]{1,0:T(8,128)(2,1)S(1)} %copy-done.3, bf16[3072,3072]{1,0:T(8,128)(2,1)} %fusion, f32[3072]{0:T(1024)S(1)} %convert_divide_fusion), kind=kOutput, calls=%fused_computation.5 | convolution fusion | flops 604176384 | bytes 19279872 | tf_op jit(solution)/shard_map/layer_one_mean/dot_general | solution.py:38
  32.0 4.1 %all-to-all-start = ((bf16[32,16,192]{2,0,1:T(8,128)(2,1)}), bf16[32,16,192]{2,0,1:T(8,128)(2,1)S(1)}, u32[]{:S(2)}, u32[]{:S(2)}) async-start(bf16[32,16,192]{2,0,1:T(8,128)(2,1)} %copy.28), calls=%async_computation | async-start | bytes 524288 | tf_op jit(solution)/shard_map/all_to_all | solution.py:140
  36.2 1.9 %collective-permute-start.7 = (bf16[32,192]{1,0:T(8,128)(2,1)S(1)}, bf16[32,192]{1,0:T(8,128)(2,1)S(1)}, u32[]{:S(2)}, u32[]{:S(2)}) collective-permute-start(bf16[32,192]{1,0:T(8,128)(2,1)S(1)} %get-tuple-element.81), channel_id=1, source_target_pairs={{0,2},{1,3},{2,0},{3,1},{4,6},{5,7},{6,4},{7,5},{8,10},{9,11},{10,... | collective-permute-start | bytes 36872 | tf_op jit(solution)/shard_map/ppermute | solution.py:18
  39.9 2.6 %collective-permute-start.11 = (bf16[32,192]{1,0:T(8,128)(2,1)S(1)}, bf16[32,192]{1,0:T(8,128)(2,1)S(1)}, u32[]{:S(2)}, u32[]{:S(2)}) collective-permute-start(bf16[32,192]{1,0:T(8,128)(2,1)S(1)} %get-tuple-element.77), channel_id=1, source_target_pairs={{0,6},{1,7},{2,4},{3,5},{4,2},{5,3},{6,0},{7,1},{8,14},{9,15},{10,... | collective-permute-start | bytes 36872 | tf_op jit(solution)/shard_map/ppermute | solution.py:18
  42.5 2.4 %collective-permute-start.13 = (bf16[32,192]{1,0:T(8,128)(2,1)S(1)}, bf16[32,192]{1,0:T(8,128)(2,1)S(1)}, u32[]{:S(2)}, u32[]{:S(2)}) collective-permute-start(bf16[32,192]{1,0:T(8,128)(2,1)S(1)} %get-tuple-element.75), channel_id=1, source_target_pairs={{0,8},{1,9},{2,10},{3,11},{4,12},{5,13},{6,14},{7,15},{8,0},{9,1},... | collective-permute-start | bytes 36872 | tf_op jit(solution)/shard_map/ppermute | solution.py:18
  45.6 3.1 %collective-permute-start.15 = (bf16[32,192]{1,0:T(8,128)(2,1)S(1)}, bf16[32,192]{1,0:T(8,128)(2,1)S(1)}, u32[]{:S(2)}, u32[]{:S(2)}) collective-permute-start(bf16[32,192]{1,0:T(8,128)(2,1)S(1)} %get-tuple-element.73), channel_id=1, source_target_pairs={{0,10},{1,11},{2,8},{3,9},{4,14},{5,15},{6,12},{7,13},{8,2},{9,3},... | collective-permute-start | bytes 36872 | tf_op jit(solution)/shard_map/ppermute | solution.py:18
  49.8 2.3 %collective-permute-start.17 = (bf16[32,192]{1,0:T(8,128)(2,1)S(1)}, bf16[32,192]{1,0:T(8,128)(2,1)S(1)}, u32[]{:S(2)}, u32[]{:S(2)}) collective-permute-start(bf16[32,192]{1,0:T(8,128)(2,1)S(1)} %get-tuple-element.71), channel_id=1, source_target_pairs={{0,12},{1,13},{2,14},{3,15},{4,8},{5,9},{6,10},{7,11},{8,4},{9,5},... | collective-permute-start | bytes 36872 | tf_op jit(solution)/shard_map/ppermute | solution.py:18
  52.7 4.0 %collective-permute-start.19 = (bf16[32,192]{1,0:T(8,128)(2,1)S(1)}, bf16[32,192]{1,0:T(8,128)(2,1)S(1)}, u32[]{:S(2)}, u32[]{:S(2)}) collective-permute-start(bf16[32,192]{1,0:T(8,128)(2,1)S(1)} %get-tuple-element.69), channel_id=1, source_target_pairs={{0,14},{1,15},{2,12},{3,13},{4,10},{5,11},{6,8},{7,9},{8,6},{9,7},... | collective-permute-start | bytes 36872 | tf_op jit(solution)/shard_map/ppermute | solution.py:18
  57.8 1.6 %collective-permute-start.4 = (bf16[2,2,192,256]{3,2,0,1:T(8,128)(2,1)S(1)}, bf16[2,2,192,256]{3,2,0,1:T(8,128)(2,1)S(1)}, u32[]{:S(2)}, u32[]{:S(2)}) collective-permute-start(bf16[2,2,192,256]{3,2,0,1:T(8,128)(2,1)S(1)} %pad_maximum_fusion.9), channel_id=1, source_target_pairs={{0,2},{1,3},{2,0},{3,1},{4,6},{5,7},{6,4},{7,5},{8,10},{9,11},{10,... | collective-permute-start | bytes 1179656 | tf_op jit(solution)/shard_map/ppermute | solution.py:45
  59.4 3.4 %collective-permute-done.20 = bf16[32,192]{1,0:T(8,128)(2,1)S(1)} collective-permute-done((bf16[32,192]{1,0:T(8,128)(2,1)S(1)}, bf16[32,192]{1,0:T(8,128)(2,1)S(1)}, u32[]{:S(2)}, u32[]{:S(2)}) %collective-permute-start.20) | collective-permute-done | bytes 12320 | tf_op jit(solution)/shard_map/ppermute | solution.py:18
  64.2 4.8 %collective-permute-done.5 = bf16[2,2,192,256]{3,2,1,0:T(8,128)(2,1)S(1)} collective-permute-done((bf16[2,2,192,256]{3,2,1,0:T(8,128)(2,1)S(1)}, bf16[2,2,192,256]{3,2,1,0:T(8,128)(2,1)S(1)}, u32[]{:S(2)}, u32[]{:S(2)}) %collective-permute-start.5) | collective-permute-done | bytes 393248 | tf_op jit(solution)/shard_map/ppermute | solution.py:45
  71.3 2.0 %collective-permute-start.21 = (bf16[192,256]{1,0:T(8,128)(2,1)S(1)}, bf16[192,256]{1,0:T(8,128)(2,1)S(1)}, u32[]{:S(2)}, u32[]{:S(2)}) collective-permute-start(bf16[192,256]{1,0:T(8,128)(2,1)S(1)} %get-tuple-element.67), channel_id=1, source_target_pairs={{0,8},{1,9},{2,10},{3,11},{4,12},{5,13},{6,14},{7,15},{8,0},{9,1},... | collective-permute-start | bytes 294920 | tf_op jit(solution)/shard_map/ppermute | solution.py:45
  76.2 2.2 %collective-permute-done.21 = bf16[192,256]{1,0:T(8,128)(2,1)S(1)} collective-permute-done((bf16[192,256]{1,0:T(8,128)(2,1)S(1)}, bf16[192,256]{1,0:T(8,128)(2,1)S(1)}, u32[]{:S(2)}, u32[]{:S(2)}) %collective-permute-start.21) | collective-permute-done | bytes 98336 | tf_op jit(solution)/shard_map/ppermute | solution.py:45
  79.7 3.0 %collective-permute-start.26 = (bf16[2,192,256]{2,1,0:T(8,128)(2,1)S(1)}, bf16[2,192,256]{2,1,0:T(8,128)(2,1)S(1)}, u32[]{:S(2)}, u32[]{:S(2)}) collective-permute-start(bf16[2,192,256]{2,1,0:T(8,128)(2,1)S(1)} %pad_maximum_fusion.16), channel_id=1, source_target_pairs={{0,8},{1,9},{2,10},{3,11},{4,12},{5,13},{6,14},{7,15},{8,0},{9,1},... | collective-permute-start | bytes 589832 | tf_op jit(solution)/shard_map/ppermute | solution.py:45
  82.7 4.5 %collective-permute-done.23 = bf16[2,192,256]{2,1,0:T(8,128)(2,1)S(1)} collective-permute-done((bf16[2,192,256]{2,1,0:T(8,128)(2,1)S(1)}, bf16[2,192,256]{2,1,0:T(8,128)(2,1)S(1)}, u32[]{:S(2)}, u32[]{:S(2)}) %collective-permute-start.23) | collective-permute-done | bytes 196640 | tf_op jit(solution)/shard_map/ppermute | solution.py:45
  88.8 3.7 %collective-permute-done.26 = bf16[2,192,256]{2,1,0:T(8,128)(2,1)S(1)} collective-permute-done((bf16[2,192,256]{2,1,0:T(8,128)(2,1)S(1)}, bf16[2,192,256]{2,1,0:T(8,128)(2,1)S(1)}, u32[]{:S(2)}, u32[]{:S(2)}) %collective-permute-start.26) | collective-permute-done | bytes 196640 | tf_op jit(solution)/shard_map/ppermute | solution.py:45
  93.0 2.1 %collective-permute-done.24 = bf16[2,2,192,256]{3,2,0,1:T(8,128)(2,1)S(1)} collective-permute-done((bf16[2,2,192,256]{3,2,0,1:T(8,128)(2,1)S(1)}, bf16[2,2,192,256]{3,2,0,1:T(8,128)(2,1)S(1)}, u32[]{:S(2)}, u32[]{:S(2)}) %collective-permute-start.24) | collective-permute-done | bytes 393248 | tf_op jit(solution)/shard_map/ppermute | solution.py:45
  95.4 8.1 %collective-permute-done.27 = bf16[2,2,192,256]{3,2,1,0:T(8,128)(2,1)S(1)} collective-permute-done((bf16[2,2,192,256]{3,2,1,0:T(8,128)(2,1)S(1)}, bf16[2,2,192,256]{3,2,1,0:T(8,128)(2,1)S(1)}, u32[]{:S(2)}, u32[]{:S(2)}) %collective-permute-start.27) | collective-permute-done | bytes 393248 | tf_op jit(solution)/shard_map/ppermute | solution.py:45
  104.5 1.6 %fusion.7 = f32[192,512]{1,0:T(8,128)S(1)} fusion(bf16[3072,256]{1,0:T(8,128)(2,1)S(1)} %bitcast.150, bf16[3072,256]{1,0:T(8,128)(2,1)S(1)} %bitcast.148, s32[3072]{0:T(1024)S(1)} %bitcast.151), kind=kOutput, calls=%fused_computation.10 | convolution fusion | flops 610861056 | bytes 3551232 | tf_op jit(solution)/shard_map/dot_general | solution.py:38
  118.1 1.6 collective-permute-start.32
  121.2 1.6 %collective-permute-start.37 = (f32[2,2,2,64,256]{4,3,2,1,0:T(8,128)S(1)}, f32[2,2,2,64,256]{4,3,2,1,0:T(8,128)S(1)}, u32[]{:S(2)}, u32[]{:S(2)}) collective-permute-start(f32[2,2,2,64,256]{4,3,2,1,0:T(8,128)S(1)} %dynamic-slice_bitcast_fusion.1), channel_id=1, source_target_pairs={{0,2},{1,3},{2,0},{3,1},{4,6},{5,7},{6,4},{7,5},{8,10},{9,11},{10,... | collective-permute-start | bytes 1572872 | tf_op jit(solution)/shard_map/weight_grad_sum/ppermute | solution.py:45
  123.7 8.7 %collective-permute-done.32 = f32[2,2,2,64,256]{4,3,2,1,0:T(8,128)S(1)} collective-permute-done((f32[2,2,2,64,256]{4,3,2,1,0:T(8,128)S(1)}, f32[2,2,2,64,256]{4,3,2,1,0:T(8,128)S(1)}, u32[]{:S(2)}, u32[]{:S(2)}) %collective-permute-start.32) | collective-permute-done | bytes 524320 | tf_op jit(solution)/shard_map/weight_grad_sum/ppermute | solution.py:45
  132.5 1.6 %collective-permute-start.33 = (f32[2,2,64,256]{3,2,1,0:T(8,128)S(1)}, f32[2,2,64,256]{3,2,1,0:T(8,128)S(1)}, u32[]{:S(2)}, u32[]{:S(2)}) collective-permute-start(f32[2,2,64,256]{3,2,1,0:T(8,128)S(1)} %dynamic-slice_bitcast_fusion.4), channel_id=1, source_target_pairs={{0,2},{1,3},{2,0},{3,1},{4,6},{5,7},{6,4},{7,5},{8,10},{9,11},{10,... | collective-permute-start | bytes 786440 | tf_op jit(solution)/shard_map/weight_grad_sum/ppermute | solution.py:45
  135.9 4.9 %collective-permute-done.33 = f32[2,2,64,256]{3,2,1,0:T(8,128)S(1)} collective-permute-done((f32[2,2,64,256]{3,2,1,0:T(8,128)S(1)}, f32[2,2,64,256]{3,2,1,0:T(8,128)S(1)}, u32[]{:S(2)}, u32[]{:S(2)}) %collective-permute-start.33) | collective-permute-done | bytes 262176 | tf_op jit(solution)/shard_map/weight_grad_sum/ppermute | solution.py:45
  143.6 5.4 %collective-permute-done.34 = f32[2,64,256]{2,1,0:T(8,128)S(1)} collective-permute-done((f32[2,64,256]{2,1,0:T(8,128)S(1)}, f32[2,64,256]{2,1,0:T(8,128)S(1)}, u32[]{:S(2)}, u32[]{:S(2)}) %collective-permute-start.34) | collective-permute-done | bytes 131104 | tf_op jit(solution)/shard_map/weight_grad_sum/ppermute | solution.py:45
  149.7 2.0 %collective-permute-start.40 = (f32[64,256]{1,0:T(8,128)S(1)}, f32[64,256]{1,0:T(8,128)S(1)}, u32[]{:S(2)}, u32[]{:S(2)}) collective-permute-start(f32[64,256]{1,0:T(8,128)S(1)} %dynamic-slice_bitcast_fusion.7), channel_id=1, source_target_pairs={{0,8},{1,9},{2,10},{3,11},{4,12},{5,13},{6,14},{7,15},{8,0},{9,1},... | collective-permute-start | bytes 196616 | tf_op jit(solution)/shard_map/weight_grad_sum/ppermute | solution.py:45
  151.7 1.8 %collective-permute-done.35 = f32[64,256]{1,0:T(8,128)S(1)} collective-permute-done((f32[64,256]{1,0:T(8,128)S(1)}, f32[64,256]{1,0:T(8,128)S(1)}, u32[]{:S(2)}, u32[]{:S(2)}) %collective-permute-start.35) | collective-permute-done | bytes 65568 | tf_op jit(solution)/shard_map/weight_grad_sum/ppermute | solution.py:45
  (175 shorter events, 43.2 us)
Async XLA Ops:
  3.0 15.6 %collective-permute-start = (bf16[192,256]{1,0:T(8,128)(2,1)S(1)}, bf16[192,256]{1,0:T(8,128)(2,1)S(1)}, u32[]{:S(2)}, u32[]{:S(2)}) collective-permute-start(bf16[192,256]{1,0:T(8,128)(2,1)S(1)} %get-tuple-element.87), channel_id=1, source_target_pairs={{0,8},{1,9},{2,10},{3,11},{4,12},{5,13},{6,14},{7,15},{8,0},{9,1},... | collective-permute-start | bytes 294920 | tf_op jit(solution)/shard_map/ppermute | solution.py:45
  7.1 11.5 %collective-permute-start.1 = (bf16[192,256]{1,0:T(8,128)(2,1)S(1)}, bf16[192,256]{1,0:T(8,128)(2,1)S(1)}, u32[]{:S(2)}, u32[]{:S(2)}) collective-permute-start(bf16[192,256]{1,0:T(8,128)(2,1)S(1)} %get-tuple-element.86), channel_id=1, source_target_pairs={{0,2},{1,3},{2,0},{3,1},{4,6},{5,7},{6,4},{7,5},{8,10},{9,11},{10,... | collective-permute-start | bytes 294920 | tf_op jit(solution)/shard_map/ppermute | solution.py:45
  18.6 11.7 %collective-permute-start.3 = (bf16[2,192,256]{2,1,0:T(8,128)(2,1)S(1)}, bf16[2,192,256]{2,1,0:T(8,128)(2,1)S(1)}, u32[]{:S(2)}, u32[]{:S(2)}) collective-permute-start(bf16[2,192,256]{2,1,0:T(8,128)(2,1)S(1)} %get-tuple-element.16), channel_id=1, source_target_pairs={{0,8},{1,9},{2,10},{3,11},{4,12},{5,13},{6,14},{7,15},{8,0},{9,1},... | collective-permute-start | bytes 589832 | tf_op jit(solution)/shard_map/layer_one_mean/ppermute | solution.py:45
  19.0 11.4 %collective-permute-start.2 = (bf16[2,192,256]{2,1,0:T(8,128)(2,1)S(1)}, bf16[2,192,256]{2,1,0:T(8,128)(2,1)S(1)}, u32[]{:S(2)}, u32[]{:S(2)}) collective-permute-start(bf16[2,192,256]{2,1,0:T(8,128)(2,1)S(1)} %get-tuple-element.15), channel_id=1, source_target_pairs={{0,4},{1,5},{2,6},{3,7},{4,0},{5,1},{6,2},{7,3},{8,12},{9,13},{10,... | collective-permute-start | bytes 589832 | tf_op jit(solution)/shard_map/layer_one_mean/ppermute | solution.py:45
  30.8 9.0 %collective-permute-start.6 = (bf16[32,192]{1,0:T(8,128)(2,1)S(1)}, bf16[32,192]{1,0:T(8,128)(2,1)S(1)}, u32[]{:S(2)}, u32[]{:S(2)}) collective-permute-start(bf16[32,192]{1,0:T(8,128)(2,1)S(1)} %get-tuple-element.82), channel_id=1, source_target_pairs={{0,1},{1,0},{2,3},{3,2},{4,5},{5,4},{6,7},{7,6},{8,9},{9,8},{10,11... | collective-permute-start | bytes 36872 | tf_op jit(solution)/shard_map/ppermute | solution.py:18
  32.0 30.8 %all-to-all-start = ((bf16[32,16,192]{2,0,1:T(8,128)(2,1)}), bf16[32,16,192]{2,0,1:T(8,128)(2,1)S(1)}, u32[]{:S(2)}, u32[]{:S(2)}) async-start(bf16[32,16,192]{2,0,1:T(8,128)(2,1)} %copy.28), calls=%async_computation | async-start | bytes 524288 | tf_op jit(solution)/shard_map/all_to_all | solution.py:140
  38.1 6.9 %collective-permute-start.9 = (bf16[32,192]{1,0:T(8,128)(2,1)S(1)}, bf16[32,192]{1,0:T(8,128)(2,1)S(1)}, u32[]{:S(2)}, u32[]{:S(2)}) collective-permute-start(bf16[32,192]{1,0:T(8,128)(2,1)S(1)} %get-tuple-element.79), channel_id=1, source_target_pairs={{0,4},{1,5},{2,6},{3,7},{4,0},{5,1},{6,2},{7,3},{8,12},{9,13},{10,... | collective-permute-start | bytes 36872 | tf_op jit(solution)/shard_map/ppermute | solution.py:18
  39.9 8.9 %collective-permute-start.11 = (bf16[32,192]{1,0:T(8,128)(2,1)S(1)}, bf16[32,192]{1,0:T(8,128)(2,1)S(1)}, u32[]{:S(2)}, u32[]{:S(2)}) collective-permute-start(bf16[32,192]{1,0:T(8,128)(2,1)S(1)} %get-tuple-element.77), channel_id=1, source_target_pairs={{0,6},{1,7},{2,4},{3,5},{4,2},{5,3},{6,0},{7,1},{8,14},{9,15},{10,... | collective-permute-start | bytes 36872 | tf_op jit(solution)/shard_map/ppermute | solution.py:18
  42.5 7.3 %collective-permute-start.12 = (bf16[32,192]{1,0:T(8,128)(2,1)S(1)}, bf16[32,192]{1,0:T(8,128)(2,1)S(1)}, u32[]{:S(2)}, u32[]{:S(2)}) collective-permute-start(bf16[32,192]{1,0:T(8,128)(2,1)S(1)} %get-tuple-element.76), channel_id=1, source_target_pairs={{0,7},{1,6},{2,5},{3,4},{4,3},{5,2},{6,1},{7,0},{8,15},{9,14},{10,... | collective-permute-start | bytes 36872 | tf_op jit(solution)/shard_map/ppermute | solution.py:18
  42.5 9.5 %collective-permute-start.13 = (bf16[32,192]{1,0:T(8,128)(2,1)S(1)}, bf16[32,192]{1,0:T(8,128)(2,1)S(1)}, u32[]{:S(2)}, u32[]{:S(2)}) collective-permute-start(bf16[32,192]{1,0:T(8,128)(2,1)S(1)} %get-tuple-element.75), channel_id=1, source_target_pairs={{0,8},{1,9},{2,10},{3,11},{4,12},{5,13},{6,14},{7,15},{8,0},{9,1},... | collective-permute-start | bytes 36872 | tf_op jit(solution)/shard_map/ppermute | solution.py:18
  45.0 7.8 %collective-permute-start.14 = (bf16[32,192]{1,0:T(8,128)(2,1)S(1)}, bf16[32,192]{1,0:T(8,128)(2,1)S(1)}, u32[]{:S(2)}, u32[]{:S(2)}) collective-permute-start(bf16[32,192]{1,0:T(8,128)(2,1)S(1)} %get-tuple-element.74), channel_id=1, source_target_pairs={{0,9},{1,8},{2,11},{3,10},{4,13},{5,12},{6,15},{7,14},{8,1},{9,0},... | collective-permute-start | bytes 36872 | tf_op jit(solution)/shard_map/ppermute | solution.py:18
  45.6 11.1 %collective-permute-start.15 = (bf16[32,192]{1,0:T(8,128)(2,1)S(1)}, bf16[32,192]{1,0:T(8,128)(2,1)S(1)}, u32[]{:S(2)}, u32[]{:S(2)}) collective-permute-start(bf16[32,192]{1,0:T(8,128)(2,1)S(1)} %get-tuple-element.73), channel_id=1, source_target_pairs={{0,10},{1,11},{2,8},{3,9},{4,14},{5,15},{6,12},{7,13},{8,2},{9,3},... | collective-permute-start | bytes 36872 | tf_op jit(solution)/shard_map/ppermute | solution.py:18
  48.7 9.0 %collective-permute-start.16 = (bf16[32,192]{1,0:T(8,128)(2,1)S(1)}, bf16[32,192]{1,0:T(8,128)(2,1)S(1)}, u32[]{:S(2)}, u32[]{:S(2)}) collective-permute-start(bf16[32,192]{1,0:T(8,128)(2,1)S(1)} %get-tuple-element.72), channel_id=1, source_target_pairs={{0,11},{1,10},{2,9},{3,8},{4,15},{5,14},{6,13},{7,12},{8,3},{9,2},... | collective-permute-start | bytes 36872 | tf_op jit(solution)/shard_map/ppermute | solution.py:18
  49.8 8.0 %collective-permute-start.17 = (bf16[32,192]{1,0:T(8,128)(2,1)S(1)}, bf16[32,192]{1,0:T(8,128)(2,1)S(1)}, u32[]{:S(2)}, u32[]{:S(2)}) collective-permute-start(bf16[32,192]{1,0:T(8,128)(2,1)S(1)} %get-tuple-element.71), channel_id=1, source_target_pairs={{0,12},{1,13},{2,14},{3,15},{4,8},{5,9},{6,10},{7,11},{8,4},{9,5},... | collective-permute-start | bytes 36872 | tf_op jit(solution)/shard_map/ppermute | solution.py:18
  52.0 7.3 %collective-permute-start.18 = (bf16[32,192]{1,0:T(8,128)(2,1)S(1)}, bf16[32,192]{1,0:T(8,128)(2,1)S(1)}, u32[]{:S(2)}, u32[]{:S(2)}) collective-permute-start(bf16[32,192]{1,0:T(8,128)(2,1)S(1)} %get-tuple-element.70), channel_id=1, source_target_pairs={{0,13},{1,12},{2,15},{3,14},{4,9},{5,8},{6,11},{7,10},{8,5},{9,4},... | collective-permute-start | bytes 36872 | tf_op jit(solution)/shard_map/ppermute | solution.py:18
  52.7 6.7 %collective-permute-start.19 = (bf16[32,192]{1,0:T(8,128)(2,1)S(1)}, bf16[32,192]{1,0:T(8,128)(2,1)S(1)}, u32[]{:S(2)}, u32[]{:S(2)}) collective-permute-start(bf16[32,192]{1,0:T(8,128)(2,1)S(1)} %get-tuple-element.69), channel_id=1, source_target_pairs={{0,14},{1,15},{2,12},{3,13},{4,10},{5,11},{6,8},{7,9},{8,6},{9,7},... | collective-permute-start | bytes 36872 | tf_op jit(solution)/shard_map/ppermute | solution.py:18
  57.8 11.2 %collective-permute-start.5 = (bf16[2,2,192,256]{3,2,1,0:T(8,128)(2,1)S(1)}, bf16[2,2,192,256]{3,2,1,0:T(8,128)(2,1)S(1)}, u32[]{:S(2)}, u32[]{:S(2)}) collective-permute-start(bf16[2,2,192,256]{3,2,1,0:T(8,128)(2,1)S(1)} %pad_maximum_fusion.10), channel_id=1, source_target_pairs={{0,4},{1,5},{2,6},{3,7},{4,0},{5,1},{6,2},{7,3},{8,12},{9,13},{10,... | collective-permute-start | bytes 1179656 | tf_op jit(solution)/shard_map/ppermute | solution.py:45
  57.8 11.3 %collective-permute-start.4 = (bf16[2,2,192,256]{3,2,0,1:T(8,128)(2,1)S(1)}, bf16[2,2,192,256]{3,2,0,1:T(8,128)(2,1)S(1)}, u32[]{:S(2)}, u32[]{:S(2)}) collective-permute-start(bf16[2,2,192,256]{3,2,0,1:T(8,128)(2,1)S(1)} %pad_maximum_fusion.9), channel_id=1, source_target_pairs={{0,2},{1,3},{2,0},{3,1},{4,6},{5,7},{6,4},{7,5},{8,10},{9,11},{10,... | collective-permute-start | bytes 1179656 | tf_op jit(solution)/shard_map/ppermute | solution.py:45
  71.3 7.1 %collective-permute-start.21 = (bf16[192,256]{1,0:T(8,128)(2,1)S(1)}, bf16[192,256]{1,0:T(8,128)(2,1)S(1)}, u32[]{:S(2)}, u32[]{:S(2)}) collective-permute-start(bf16[192,256]{1,0:T(8,128)(2,1)S(1)} %get-tuple-element.67), channel_id=1, source_target_pairs={{0,8},{1,9},{2,10},{3,11},{4,12},{5,13},{6,14},{7,15},{8,0},{9,1},... | collective-permute-start | bytes 294920 | tf_op jit(solution)/shard_map/ppermute | solution.py:45
  78.5 8.7 %collective-permute-start.23 = (bf16[2,192,256]{2,1,0:T(8,128)(2,1)S(1)}, bf16[2,192,256]{2,1,0:T(8,128)(2,1)S(1)}, u32[]{:S(2)}, u32[]{:S(2)}) collective-permute-start(bf16[2,192,256]{2,1,0:T(8,128)(2,1)S(1)} %pad_maximum_fusion.15), channel_id=1, source_target_pairs={{0,4},{1,5},{2,6},{3,7},{4,0},{5,1},{6,2},{7,3},{8,12},{9,13},{10,... | collective-permute-start | bytes 589832 | tf_op jit(solution)/shard_map/ppermute | solution.py:45
  79.6 24.1 %collective-permute-start.29 = (bf16[2,2,2,192,256]{4,3,0,1,2:T(8,128)(2,1)S(1)}, bf16[2,2,2,192,256]{4,3,0,1,2:T(8,128)(2,1)S(1)}, u32[]{:S(2)}, u32[]{:S(2)}) collective-permute-start(bf16[2,2,2,192,256]{4,3,0,1,2:T(8,128)(2,1)S(1)} %pad_maximum_fusion.5), channel_id=1, source_target_pairs={{0,1},{1,0},{2,3},{3,2},{4,5},{5,4},{6,7},{7,6},{8,9},{9,8},{10,11... | collective-permute-start | bytes 2359304 | tf_op jit(solution)/shard_map/ppermute | solution.py:45
  79.7 12.8 %collective-permute-start.26 = (bf16[2,192,256]{2,1,0:T(8,128)(2,1)S(1)}, bf16[2,192,256]{2,1,0:T(8,128)(2,1)S(1)}, u32[]{:S(2)}, u32[]{:S(2)}) collective-permute-start(bf16[2,192,256]{2,1,0:T(8,128)(2,1)S(1)} %pad_maximum_fusion.16), channel_id=1, source_target_pairs={{0,8},{1,9},{2,10},{3,11},{4,12},{5,13},{6,14},{7,15},{8,0},{9,1},... | collective-permute-start | bytes 589832 | tf_op jit(solution)/shard_map/ppermute | solution.py:45
  87.3 7.8 %collective-permute-start.24 = (bf16[2,2,192,256]{3,2,0,1:T(8,128)(2,1)S(1)}, bf16[2,2,192,256]{3,2,0,1:T(8,128)(2,1)S(1)}, u32[]{:S(2)}, u32[]{:S(2)}) collective-permute-start(bf16[2,2,192,256]{3,2,0,1:T(8,128)(2,1)S(1)} %pad_maximum_fusion.11), channel_id=1, source_target_pairs={{0,2},{1,3},{2,0},{3,1},{4,6},{5,7},{6,4},{7,5},{8,10},{9,11},{10,... | collective-permute-start | bytes 1179656 | tf_op jit(solution)/shard_map/ppermute | solution.py:45
  92.5 10.9 %collective-permute-start.27 = (bf16[2,2,192,256]{3,2,1,0:T(8,128)(2,1)S(1)}, bf16[2,2,192,256]{3,2,1,0:T(8,128)(2,1)S(1)}, u32[]{:S(2)}, u32[]{:S(2)}) collective-permute-start(bf16[2,2,192,256]{3,2,1,0:T(8,128)(2,1)S(1)} %pad_maximum_fusion.12), channel_id=1, source_target_pairs={{0,4},{1,5},{2,6},{3,7},{4,0},{5,1},{6,2},{7,3},{8,12},{9,13},{10,... | collective-permute-start | bytes 1179656 | tf_op jit(solution)/shard_map/ppermute | solution.py:45
  93.0 11.1 %collective-permute-start.30 = (bf16[2,2,2,192,256]{4,3,2,0,1:T(8,128)(2,1)S(1)}, bf16[2,2,2,192,256]{4,3,2,0,1:T(8,128)(2,1)S(1)}, u32[]{:S(2)}, u32[]{:S(2)}) collective-permute-start(bf16[2,2,2,192,256]{4,3,2,0,1:T(8,128)(2,1)S(1)} %pad_maximum_fusion.6), channel_id=1, source_target_pairs={{0,1},{1,0},{2,3},{3,2},{4,5},{5,4},{6,7},{7,6},{8,9},{9,8},{10,11... | collective-permute-start | bytes 2359304 | tf_op jit(solution)/shard_map/ppermute | solution.py:45
  95.3 11.8 %collective-permute-start.25 = (bf16[2,2,2,192,256]{4,3,0,1,2:T(8,128)(2,1)S(1)}, bf16[2,2,2,192,256]{4,3,0,1,2:T(8,128)(2,1)S(1)}, u32[]{:S(2)}, u32[]{:S(2)}) collective-permute-start(bf16[2,2,2,192,256]{4,3,0,1,2:T(8,128)(2,1)S(1)} %pad_maximum_fusion.7), channel_id=1, source_target_pairs={{0,1},{1,0},{2,3},{3,2},{4,5},{5,4},{6,7},{7,6},{8,9},{9,8},{10,11... | collective-permute-start | bytes 2359304 | tf_op jit(solution)/shard_map/ppermute | solution.py:45
  118.1 14.3 %collective-permute-start.32 = (f32[2,2,2,64,256]{4,3,2,1,0:T(8,128)S(1)}, f32[2,2,2,64,256]{4,3,2,1,0:T(8,128)S(1)}, u32[]{:S(2)}, u32[]{:S(2)}) collective-permute-start(f32[2,2,2,64,256]{4,3,2,1,0:T(8,128)S(1)} %dynamic-slice_bitcast_fusion.2), channel_id=1, source_target_pairs={{0,16},{16,0},{1,17},{17,1},{2,18},{18,2},{3,19},{19,3},{4,20},{20... | collective-permute-start | bytes 1572872 | tf_op jit(solution)/shard_map/weight_grad_sum/ppermute | solution.py:45
  121.2 14.4 %collective-permute-start.37 = (f32[2,2,2,64,256]{4,3,2,1,0:T(8,128)S(1)}, f32[2,2,2,64,256]{4,3,2,1,0:T(8,128)S(1)}, u32[]{:S(2)}, u32[]{:S(2)}) collective-permute-start(f32[2,2,2,64,256]{4,3,2,1,0:T(8,128)S(1)} %dynamic-slice_bitcast_fusion.1), channel_id=1, source_target_pairs={{0,2},{1,3},{2,0},{3,1},{4,6},{5,7},{6,4},{7,5},{8,10},{9,11},{10,... | collective-permute-start | bytes 1572872 | tf_op jit(solution)/shard_map/weight_grad_sum/ppermute | solution.py:45
  132.5 8.3 %collective-permute-start.33 = (f32[2,2,64,256]{3,2,1,0:T(8,128)S(1)}, f32[2,2,64,256]{3,2,1,0:T(8,128)S(1)}, u32[]{:S(2)}, u32[]{:S(2)}) collective-permute-start(f32[2,2,64,256]{3,2,1,0:T(8,128)S(1)} %dynamic-slice_bitcast_fusion.4), channel_id=1, source_target_pairs={{0,2},{1,3},{2,0},{3,1},{4,6},{5,7},{6,4},{7,5},{8,10},{9,11},{10,... | collective-permute-start | bytes 786440 | tf_op jit(solution)/shard_map/weight_grad_sum/ppermute | solution.py:45
  135.7 7.3 %collective-permute-start.38 = (f32[2,2,64,256]{3,2,1,0:T(8,128)S(1)}, f32[2,2,64,256]{3,2,1,0:T(8,128)S(1)}, u32[]{:S(2)}, u32[]{:S(2)}) collective-permute-start(f32[2,2,64,256]{3,2,1,0:T(8,128)S(1)} %dynamic-slice_bitcast_fusion.3), channel_id=1, source_target_pairs={{0,16},{16,0},{1,17},{17,1},{2,18},{18,2},{3,19},{19,3},{4,20},{20... | collective-permute-start | bytes 786440 | tf_op jit(solution)/shard_map/weight_grad_sum/ppermute | solution.py:45
  140.9 8.1 %collective-permute-start.34 = (f32[2,64,256]{2,1,0:T(8,128)S(1)}, f32[2,64,256]{2,1,0:T(8,128)S(1)}, u32[]{:S(2)}, u32[]{:S(2)}) collective-permute-start(f32[2,64,256]{2,1,0:T(8,128)S(1)} %dynamic-slice_bitcast_fusion.6), channel_id=1, source_target_pairs={{0,8},{1,9},{2,10},{3,11},{4,12},{5,13},{6,14},{7,15},{8,0},{9,1},... | collective-permute-start | bytes 393224 | tf_op jit(solution)/shard_map/weight_grad_sum/ppermute | solution.py:45
  143.0 6.7 %collective-permute-start.39 = (f32[2,64,256]{2,1,0:T(8,128)S(1)}, f32[2,64,256]{2,1,0:T(8,128)S(1)}, u32[]{:S(2)}, u32[]{:S(2)}) collective-permute-start(f32[2,64,256]{2,1,0:T(8,128)S(1)} %dynamic-slice_bitcast_fusion.5), channel_id=1, source_target_pairs={{0,4},{1,5},{2,6},{3,7},{4,0},{5,1},{6,2},{7,3},{8,12},{9,13},{10,... | collective-permute-start | bytes 393224 | tf_op jit(solution)/shard_map/weight_grad_sum/ppermute | solution.py:45
  (21 other events, 75.7 us)
